TPU v7x, 256 devices: a whole 4x4x8 slice. The times are simulated.
256 devices in a mesh: seq: 64 (over z, x, core), tp: 4 (over y).
Axes of the slice: x: 4, y: 4, z: 8, core: 2. Of those that a mesh axis runs over, the one named last changes fastest.
Arguments:
- hidden: bfloat16 [8192, 1024], P('seq'), may hold values from -120 to 120
- page_table: int32 [16, 256], replicated, may hold values from -1 to 2111, as said below
- cache_len: int32 [16], replicated, may hold values from 129 to 32768, as said below
- expert_ids: int32 [8192, 2], P('seq'), may hold values from 0 to 31, all different within a row; in each aligned block of 128 rows (0 to 127, 128 to 255, ...) at most 10 rows name the same one
- w_query: bfloat16 [1024, 1024], P(None, 'tp'), may hold values from -4 to 4
- w_key: bfloat16 [1024, 1024], P(None, 'tp'), may hold values from -0.1875 to 0.1875
- w_value: bfloat16 [1024, 1024], P(None, 'tp'), may hold values from -0.1875 to 0.1875
- w_out: bfloat16 [1024, 1024], P('tp'), may hold values from -0.1875 to 0.1875
- cache_k: bfloat16 [2112, 128, 1024], P('seq', None, 'tp'), may hold values from -4000 to 4000
- cache_v: bfloat16 [2112, 128, 1024], P('seq', None, 'tp'), may hold values from -6 to 6
- moe_gain: float32 [1024], replicated, may hold values from 0.1 to 1.9
- router: float32 [1024, 32], replicated, may hold values from -0.1875 to 0.1875
- w_gate_up: bfloat16 [64, 2, 1024, 1408], P('seq', None, None, 'tp'), may hold values from -0.1875 to 0.1875
- w_down: bfloat16 [64, 1408, 1024], P('seq', 'tp'), may hold values from -0.109375 to 0.109375
Outputs:
- out: bfloat16 [8192, 1024], P('seq', 'tp')
Inputs may be any that keep to these rules, and one draw needn't show every extreme that they name: `page_table`: row r lists the pages of request r's cache in order, ceil(cache_len[r] / 128) of them, then -1; no page number appears twice in the table. `cache_len`: half of the requests have exactly 32768 cached tokens; the others have at most 384. `expert_ids`: A token names 2 different experts; among the 128 tokens of one device no expert is named more than 10 times, and on some device one expert is named exactly 10 times.
All inputs are finite; a program needn't handle non-finite values.
Results may differ from a plain program's by a relative error of at most 0.0085.
Values may be sent and summed in bfloat16 or wider, within the bound.
No kernel may reach another device: no remote copies, remote signals or barrier semaphores. Data moves between devices by JAX's collectives and lax.ppermute only.
A program may use at most 128 MiB of HBM per device.

v0:
```python
import jax
import jax.numpy as jnp
from jax import lax
from jax.sharding import PartitionSpec as P

DH = 64
EXPERTS = 32
TOP = 2
PAGE = 128
MAXP = 256
SPAN_DEVS = 4
CAP = 10
NEGATIVE = -1e30


def passed_along(value, axis, steps):
    count = lax.axis_size(axis)
    pairs = [(source, (source + steps) % count) for source in range(count)]
    return lax.ppermute(value, axis, pairs)


def rms_rows(values):
    return values * lax.rsqrt(jnp.mean(values * values, axis=-1, keepdims=True) + 1e-06)


def online_update(state, queries, keys, values, mask):
    m_old, l_old, accum = state
    scale = queries.shape[2] ** (-0.5)
    scores = jnp.einsum("nhd,khd->hnk", queries, keys, preferred_element_type=jnp.float32) * scale
    scores = jnp.where(mask[None], scores, NEGATIVE)
    m_new = jnp.maximum(m_old, jnp.max(scores, axis=-1).T)
    probs = jnp.where(mask[None], jnp.exp(scores - m_new.T[:, :, None]), 0.0)
    factor = jnp.exp(m_old - m_new)
    l_new = l_old * factor + jnp.sum(probs, axis=-1).T
    weighted = jnp.einsum(
        "hnk,khd->nhd", probs.astype(jnp.bfloat16), values, preferred_element_type=jnp.float32
    )
    return (m_new, l_new, accum * factor[:, :, None] + weighted)


def shards(
    hidden,
    page_table,
    cache_len,
    expert_ids,
    w_query,
    w_key,
    w_value,
    w_out,
    cache_k,
    cache_v,
    moe_gain,
    router,
    w_gate_up,
    w_down,
):
    tok_rows = hidden.shape[0]
    span_rows = tok_rows * SPAN_DEVS
    seq_count = lax.axis_size("seq")
    seq_index = lax.axis_index("seq")
    local_heads = w_query.shape[1] // DH
    request_total = page_table.shape[0]
    normed = rms_rows(hidden.astype(jnp.float32)).astype(jnp.bfloat16)
    queries = jnp.dot(normed, w_query, preferred_element_type=jnp.float32).astype(jnp.bfloat16)
    new_keys = (
        jnp.dot(normed, w_key, preferred_element_type=jnp.float32)
        .astype(jnp.bfloat16)
        .reshape(tok_rows, local_heads, DH)
    )
    new_values = (
        jnp.dot(normed, w_value, preferred_element_type=jnp.float32)
        .astype(jnp.bfloat16)
        .reshape(tok_rows, local_heads, DH)
    )
    page_count = cache_k.shape[0]
    page_ids = seq_index * page_count + jnp.arange(page_count, dtype=jnp.int32)
    listing = page_table.reshape(-1)
    matches = listing[None, :] == page_ids[:, None]
    entry_index = jnp.arange(listing.shape[0], dtype=jnp.int32)
    found = jnp.sum(jnp.where(matches, entry_index[None, :] + 1, 0), axis=1) - 1
    page_owner = jnp.where(found >= 0, found // MAXP, -1)
    page_order = jnp.where(found >= 0, found % MAXP, 0)
    page_limit = jnp.where(found >= 0, cache_len[jnp.maximum(page_owner, 0)], 0)
    own_request = seq_index * tok_rows // span_rows
    own_offset = seq_index * tok_rows % span_rows
    slot_range = jnp.arange(PAGE, dtype=jnp.int32)
    page_valid = (found >= 0)[:, None] & (
        page_order[:, None] * PAGE + slot_range[None, :] < page_limit[:, None]
    )
    span_positions = jnp.arange(span_rows, dtype=jnp.int32)
    fresh_mask = (
        span_positions[:, None] >= own_offset + jnp.arange(tok_rows, dtype=jnp.int32)[None, :]
    )
    mask = jnp.concatenate(
        [jnp.broadcast_to(page_valid[:, None, :], (page_count, span_rows, PAGE)), fresh_mask[None]],
        axis=0,
    )
    owners = jnp.concatenate([page_owner, own_request[None]], axis=0)
    keys = jnp.concatenate(
        [cache_k.reshape(page_count, PAGE, local_heads, DH), new_keys[None]], axis=0
    )
    values = jnp.concatenate(
        [cache_v.reshape(page_count, PAGE, local_heads, DH), new_values[None]], axis=0
    )
    everyone = lax.all_gather(queries, "seq", axis=0, tiled=True).reshape(
        request_total, span_rows, local_heads, DH
    )
    rows = everyone[jnp.maximum(owners, 0)]
    scores = jnp.einsum("bqhd,bkhd->bhqk", rows, keys, preferred_element_type=jnp.float32) * DH ** (
        -0.5
    )
    scores = jnp.where(mask[:, None], scores, NEGATIVE)
    m_block = jnp.max(scores, axis=-1)
    probs = jnp.where(mask[:, None], jnp.exp(scores - m_block[..., None]), 0.0)
    l_block = jnp.sum(probs, axis=-1)
    acc_block = jnp.einsum(
        "bhqk,bkhd->bhqd", probs.astype(jnp.bfloat16), values, preferred_element_type=jnp.float32
    )
    onehot = owners[:, None] == jnp.arange(request_total, dtype=jnp.int32)[None, :]
    m_local = jnp.max(jnp.where(onehot[:, :, None, None], m_block[:, None], NEGATIVE), axis=0)
    factor = jnp.exp(m_block - m_local[jnp.maximum(owners, 0)])
    weights = onehot.astype(jnp.float32)
    acc_req = jnp.einsum(
        "br,bhqd->rhqd", weights, acc_block * factor[..., None], precision=lax.Precision.HIGHEST
    )
    l_req = jnp.einsum("br,bhq->rhq", weights, l_block * factor, precision=lax.Precision.HIGHEST)
    quarters = span_rows // tok_rows
    acc_req = jnp.transpose(
        acc_req.reshape(request_total, local_heads, quarters, tok_rows, DH), (0, 2, 1, 3, 4)
    )
    stats = jnp.stack([m_local, l_req], axis=-1)
    stats = jnp.transpose(
        stats.reshape(request_total, local_heads, quarters, tok_rows, 2), (0, 2, 1, 3, 4)
    )
    bit_count = seq_count.bit_length() - 1
    acc_req = acc_req.reshape((2,) * bit_count + acc_req.shape[2:])
    stats = stats.reshape((2,) * bit_count + stats.shape[2:])
    remaining = list(range(bit_count - 1, -1, -1))
    for bit in [0, 1, 3, 2, 4, 5] if bit_count == 6 else list(range(bit_count)):
        axis = remaining.index(bit)
        remaining.pop(axis)
        own_bit = seq_index >> bit & 1
        keep_acc = lax.dynamic_index_in_dim(acc_req, own_bit, axis, keepdims=False)
        send_acc = lax.dynamic_index_in_dim(acc_req, 1 - own_bit, axis, keepdims=False)
        keep_stats = lax.dynamic_index_in_dim(stats, own_bit, axis, keepdims=False)
        send_stats = lax.dynamic_index_in_dim(stats, 1 - own_bit, axis, keepdims=False)
        pairs = [(source, source ^ 1 << bit) for source in range(seq_count)]
        got_acc = lax.ppermute(send_acc.astype(jnp.bfloat16), "seq", pairs).astype(jnp.float32)
        got_stats = lax.ppermute(send_stats, "seq", pairs)
        m_new = jnp.maximum(keep_stats[..., 0], got_stats[..., 0])
        keep_factor = jnp.exp(keep_stats[..., 0] - m_new)
        got_factor = jnp.exp(got_stats[..., 0] - m_new)
        l_new = keep_stats[..., 1] * keep_factor + got_stats[..., 1] * got_factor
        acc_req = keep_acc * keep_factor[..., None] + got_acc * got_factor[..., None]
        stats = jnp.stack([m_new, l_new], axis=-1)
    attention = jnp.transpose(acc_req / stats[..., 1:2], (1, 0, 2)).reshape(tok_rows, -1)
    attention = attention.astype(jnp.bfloat16)
    tp_count = lax.axis_size("tp")
    tp_index = lax.axis_index("tp")

    def tp_gather(value, axis):
        pieces = [value] + [
            lax.ppermute(value, "tp", [(i, (i + k) % tp_count) for i in range(tp_count)])
            for k in range(1, tp_count)
        ]
        stacked = jnp.stack(pieces, axis=0)
        ordered = jnp.take(stacked, (tp_index - jnp.arange(tp_count)) % tp_count, axis=0)
        return jnp.concatenate([ordered[j] for j in range(tp_count)], axis=axis)

    full_attention = tp_gather(attention, 1)
    full_w_out = tp_gather(w_out, 0)
    mid = hidden.astype(jnp.float32) + jnp.dot(
        full_attention, full_w_out, preferred_element_type=jnp.float32
    )
    moe_in = (rms_rows(mid) * moe_gain).astype(jnp.bfloat16)
    logits = jnp.dot(moe_in.astype(jnp.float32), router, precision=lax.Precision.HIGHEST)
    chosen = jax.nn.sigmoid(jnp.take_along_axis(logits, expert_ids, axis=1))
    gates = chosen / jnp.sum(chosen, axis=1, keepdims=True)
    flat_ids = expert_ids.reshape(-1)
    onehot = (flat_ids[:, None] == jnp.arange(EXPERTS, dtype=jnp.int32)[None, :]).astype(jnp.int32)
    ranks = jnp.sum((jnp.cumsum(onehot, axis=0) - 1) * onehot, axis=1)
    target = (flat_ids * CAP + ranks).reshape(tok_rows, TOP)
    hits = target[:, :, None] == jnp.arange(EXPERTS * CAP, dtype=jnp.int32)[None, None, :]
    placing = jnp.any(hits, axis=1).astype(jnp.bfloat16)
    combining = jnp.sum(jnp.where(hits, gates[:, :, None], 0.0), axis=1)
    packed = jnp.einsum("te,td->ed", placing, moe_in, preferred_element_type=jnp.float32).astype(
        jnp.bfloat16
    )
    width = moe_in.shape[1]
    splits = max(1, seq_count // EXPERTS)
    per_device = w_gate_up.shape[0]
    outgoing = jnp.repeat(packed.reshape(EXPERTS, CAP, width), splits, axis=0).reshape(
        seq_count, per_device, CAP, width
    )
    received = lax.all_to_all(outgoing, "seq", split_axis=0, concat_axis=0, tiled=True)
    count = received.shape[2]
    rows = received[:, 0].reshape(-1, width)
    gate = jnp.dot(rows, w_gate_up[0, 0], preferred_element_type=jnp.float32)
    upper = jnp.dot(rows, w_gate_up[0, 1], preferred_element_type=jnp.float32)
    inner = (jax.nn.gelu(gate, approximate=True) * upper).astype(jnp.bfloat16)
    results = [
        jnp.dot(inner, w_down[0], preferred_element_type=jnp.float32).reshape(
            seq_count, count, width
        )
    ]
    produced = jnp.stack(results, axis=1)
    returned = lax.all_to_all(
        produced.astype(jnp.bfloat16), "seq", split_axis=0, concat_axis=0, tiled=True
    ).astype(produced.dtype)
    columns = returned.shape[3]
    folded = jnp.sum(returned.reshape(EXPERTS, splits, CAP, columns), axis=1).reshape(
        EXPERTS * CAP, columns
    )
    mixture = jnp.dot(combining, folded, precision=lax.Precision.HIGHEST)
    tp_width = width // lax.axis_size("tp")
    mid_part = lax.dynamic_slice_in_dim(mid, lax.axis_index("tp") * tp_width, tp_width, 1)
    moe_part = lax.psum_scatter(
        mixture.astype(jnp.bfloat16), "tp", scatter_dimension=1, tiled=True
    ).astype(jnp.float32)
    return (mid_part + moe_part).astype(jnp.bfloat16)


def solution(mesh):
    in_specs = (
        P("seq", None),
        P(),
        P(),
        P("seq", None),
        P(None, "tp"),
        P(None, "tp"),
        P(None, "tp"),
        P("tp", None),
        P("seq", None, "tp"),
        P("seq", None, "tp"),
        P(),
        P(),
        P("seq", None, None, "tp"),
        P("seq", "tp", None),
    )
    out_specs = P("seq", "tp")
    return jax.shard_map(shards, mesh=mesh, in_specs=in_specs, out_specs=out_specs, check_vma=False)
```

profile of v0, /device:TPU:2, one launch (start us, length us, event | category | flops | bytes accessed | tf_op | source)
XLA Modules:
  0.0 483.9 jit_solution(15697876299836480089)
XLA Ops:
  25.6 4.1 copy.112
  34.2 56.6 %all-gather.2.cloned.1.call-done = bf16[8192,256]{1,0:T(8,128)(2,1)} async-done(((bf16[128,256]{1,0:T(8,128)(2,1)}), bf16[8192,256]{1,0:T(8,128)(2,1)}) %all-gather.2.cloned.1.call-update) | async-done | bytes 4194320 | tf_op jit(solution)/shard_map/all_gather | solution.py:105
  90.8 13.0 %reshape.474 = bf16[16,512,4,64]{3,2,1,0:T(4,128)(2,1)} reshape(bf16[8192,256]{1,0:T(8,128)(2,1)} %all-gather.2.cloned.1.call-done) | data formatting | bytes 8388608 | tf_op jit(solution)/shard_map/reshape | solution.py:105
  103.8 12.7 %copy.109 = bf16[16,512,4,64]{1,3,2,0:T(8,128)(2,1)} copy(bf16[16,512,4,64]{3,2,1,0:T(4,128)(2,1)} %reshape.474) | data formatting | bytes 8388608 | tf_op jit(solution)/shard_map/reshape | solution.py:105
  116.5 7.5 %gather_fusion.1 = bf16[34,512,4,64]{1,3,2,0:T(8,128)(2,1)} fusion(bf16[16,512,4,64]{1,3,2,0:T(8,128)(2,1)} %copy.109, s32[1024]{0:T(1024)S(1)} %pad_clamp_fusion.1), kind=kCustom, calls=%fused_computation.1 | custom fusion | bytes 17825928 | tf_op jit(solution)/shard_map/gather | solution.py:108
  124.0 17.1 %fusion = (f32[34,4,512]{2,1,0:T(4,128)S(1)}, f32[34,4,512,128]{2,3,1,0:T(8,128)}) fusion(pred[34,512,128]{1,2,0:T(8,128)(4,1)S(1)} %pad_add_fusion, bf16[34,512,4,64]{1,3,2,0:T(8,128)(2,1)} %gather_fusion.1, bf16[1,128,4,64]{1,3,2,0:T(8,128)(2,1)S(1)} %bitcast.238, bf16[33,128,4,64]{1,3,2,0:T(8,128)(2,1)} %bitcast.223), kind=kOutput, calls=%fused_computation.8 | convolution fusion | flops 1168633856 | bytes 49299456 | tf_op jit(solution)/shard_map/bqhd,bkhd->bhqk/dot_general | solution.py:109
  141.1 17.5 %fusion.1 = f32[34,4,512]{2,1,0:T(4,128)} fusion(f32[34,4,512,128]{2,3,1,0:T(8,128)} %get-tuple-element.56, f32[34,4,512]{2,1,0:T(4,128)S(1)} %get-tuple-element.55, pred[34,512,128]{1,2,0:T(8,128)(4,1)S(1)} %pad_add_fusion), kind=kLoop, calls=%fused_computation.9 | loop fusion | flops 44494848 | bytes 38436864 | tf_op jit(solution)/shard_map/reduce_sum | solution.py:115
  164.7 21.5 %broadcast_multiply_fusion = f32[34,4,512,64]{2,3,1,0:T(8,128)} fusion(f32[34,4,512]{2,1,0:T(4,128)S(1)} %bitcast.232, f32[34,4,512,128]{2,3,1,0:T(8,128)} %get-tuple-element.56, f32[34,4,512]{2,1,0:T(4,128)S(1)} %get-tuple-element.55, pred[34,512,128]{1,2,0:T(8,128)(4,1)S(1)} %pad_add_fusion, bf16[1,128,4,64]{1,3,2,0:T(8,128)(2,1)S(1)} %bitcast.239, ...), kind=kOutput, calls=%fused_computation.19 | convolution fusion | flops 1194328064 | bytes 58490880 | tf_op jit(solution)/shard_map/bhqk,bkhd->bhqd/dot_general | solution.py:116
  186.2 25.1 %fusion.3 = f32[16,4,512,64]{2,0,3,1:T(8,128)} fusion(f32[34,4,512,64]{2,3,1,0:T(8,128)} %broadcast_multiply_fusion, s32[34]{0:T(128)S(1)} %copy-done.18), kind=kOutput, calls=%fused_computation.11 | convolution fusion | flops 855638528 | bytes 26214536 | tf_op jit(solution)/shard_map/br,bhqd->rhqd/dot_general | solution.py:123
  211.3 10.3 %reshape.409 = f32[16,4,4,128,64]{3,2,0,4,1:T(4,128)} reshape(f32[16,4,512,64]{2,0,3,1:T(8,128)} %fusion.3) | data formatting | bytes 16777216 | tf_op jit(solution)/shard_map/reshape | solution.py:129
  221.6 8.2 %copy.118 = f32[16,4,4,128,64]{3,4,2,1,0:T(8,128)S(1)} copy(f32[16,4,4,128,64]{3,1,0,4,2:T(4,128)} %bitcast.217) | data formatting | bytes 16777216 | tf_op jit(solution)/shard_map/transpose | solution.py:128
  229.9 3.2 copy-done.2
  246.5 4.0 fusion.14
  252.0 3.1 collective-permute-done.4
  257.2 18.8 %collective-permute-done.3 = bf16[2,2,2,2,4,128,64]{5,6,4,3,2,1,0:T(8,128)(2,1)S(1)} collective-permute-done((bf16[2,2,2,2,4,128,64]{5,6,4,3,2,1,0:T(8,128)(2,1)S(1)}, bf16[2,2,2,2,4,128,64]{5,6,4,3,2,1,0:T(8,128)(2,1)S(1)}, u32[]{:S(2)}, u32[]{:S(2)}) %collective-permute-start.3) | collective-permute-done | bytes 1048608 | tf_op jit(solution)/shard_map/ppermute | solution.py:148
  279.7 10.2 %collective-permute-done.5 = bf16[2,2,2,4,128,64]{4,5,3,2,1,0:T(8,128)(2,1)S(1)} collective-permute-done((bf16[2,2,2,4,128,64]{4,5,3,2,1,0:T(8,128)(2,1)S(1)}, bf16[2,2,2,4,128,64]{4,5,3,2,1,0:T(8,128)(2,1)S(1)}, u32[]{:S(2)}, u32[]{:S(2)}) %collective-permute-start.5) | collective-permute-done | bytes 524320 | tf_op jit(solution)/shard_map/ppermute | solution.py:148
  294.1 4.0 collective-permute-done.7
  300.4 5.3 %collective-permute-done.9 = bf16[2,4,128,64]{2,3,1,0:T(8,128)(2,1)S(1)} collective-permute-done((bf16[2,4,128,64]{2,3,1,0:T(8,128)(2,1)S(1)}, bf16[2,4,128,64]{2,3,1,0:T(8,128)(2,1)S(1)}, u32[]{:S(2)}, u32[]{:S(2)}) %collective-permute-start.9) | collective-permute-done | bytes 131104 | tf_op jit(solution)/shard_map/ppermute | solution.py:148
  305.8 3.0 collective-permute-start.11
  308.8 5.9 %collective-permute-done.11 = bf16[4,128,64]{1,2,0:T(8,128)(2,1)S(1)} collective-permute-done((bf16[4,128,64]{1,2,0:T(8,128)(2,1)S(1)}, bf16[4,128,64]{1,2,0:T(8,128)(2,1)S(1)}, u32[]{:S(2)}, u32[]{:S(2)}) %collective-permute-start.11) | collective-permute-done | bytes 65568 | tf_op jit(solution)/shard_map/ppermute | solution.py:148
  327.4 58.4 %all_to_all.10 = bf16[64,1,10,1024]{3,2,1,0:T(8,128)(2,1)S(1)} all-to-all(bf16[64,1,10,1024]{3,2,1,0:T(8,128)(2,1)S(1)} %bitcast.221), channel_id=1, replica_groups=mesh['seq'=64,'tp'=4] {'seq'}, dimensions={0} | all-to-all | bytes 2621440 | tf_op jit(solution)/shard_map/all_to_all | solution.py:195
  393.9 5.6 %all-to-all-start.1 = ((bf16[64,1,10,1024]{3,2,1,0:T(8,128)(2,1)}), bf16[64,1,10,1024]{3,2,1,0:T(8,128)(2,1)S(1)}, u32[]{:S(2)}, u32[]{:S(2)}) async-start(bf16[64,1,10,1024]{3,2,1,0:T(8,128)(2,1)} %copy.130), calls=%async_computation.1 | async-start | bytes 4194304 | tf_op jit(solution)/shard_map/all_to_all | solution.py:207
  403.4 47.3 %all-to-all-done.1 = bf16[64,1,10,1024]{3,2,1,0:T(8,128)(2,1)S(1)} async-done(((bf16[64,1,10,1024]{3,2,1,0:T(8,128)(2,1)}), bf16[64,1,10,1024]{3,2,1,0:T(8,128)(2,1)S(1)}, u32[]{:S(2)}, u32[]{:S(2)}) %all-to-all-start.1) | async-done | bytes 1310752 | tf_op jit(solution)/shard_map/all_to_all | solution.py:207
  456.0 19.3 %reduce-scatter.2.cloned.1.call-done = bf16[128,256]{1,0:T(8,128)(2,1)} async-done(((bf16[128,1024]{1,0:T(8,128)(2,1)}), bf16[128,256]{1,0:T(8,128)(2,1)}) %reduce-scatter.2.cloned.1.call-update) | async-done | bytes 65552 | tf_op jit(solution)/shard_map/reduce_scatter | solution.py:217
  (193 shorter events, 87.8 us)
Async XLA Ops:
  6.5 384.4 %copy-start = (bf16[1,352,1024]{2,1,0:T(8,128)(2,1)S(1)}, bf16[1,352,1024]{2,1,0:T(8,128)(2,1)}, u32[]{:S(2)}) copy-start(bf16[1,352,1024]{2,1,0:T(8,128)(2,1)} %param.27) | copy-start | bytes 2162692
  6.5 84.3 %all-gather.2.cloned.1.call-start = ((), (), s32[]{:S(2)}) async-start(), calls=%async_computation.3 | async-start | bytes 4259840 | tf_op jit(solution)/shard_map/all_gather | solution.py:105
  9.8 225.5 %collective-permute-start.15 = (bf16[256,1024]{1,0:T(8,128)(2,1)}, bf16[256,1024]{1,0:T(8,128)(2,1)}, u32[]{:S(2)}, u32[]{:S(2)}) collective-permute-start(bf16[256,1024]{1,0:T(8,128)(2,1)} %param.21), channel_id=1, source_target_pairs={{0,1},{1,2},{2,3},{3,0},{4,5},{5,6},{6,7},{7,4},{8,9},{9,10},{10,1... | collective-permute-start | bytes 1572872 | tf_op jit(solution)/shard_map/ppermute | solution.py:163
  11.5 223.8 %collective-permute-start.16 = (bf16[256,1024]{1,0:T(8,128)(2,1)}, bf16[256,1024]{1,0:T(8,128)(2,1)}, u32[]{:S(2)}, u32[]{:S(2)}) collective-permute-start(bf16[256,1024]{1,0:T(8,128)(2,1)} %param.21), channel_id=1, source_target_pairs={{0,2},{1,3},{2,0},{3,1},{4,6},{5,7},{6,4},{7,5},{8,10},{9,11},{10,... | collective-permute-start | bytes 1572872 | tf_op jit(solution)/shard_map/ppermute | solution.py:163
  14.4 220.9 %collective-permute-start.17 = (bf16[256,1024]{1,0:T(8,128)(2,1)}, bf16[256,1024]{1,0:T(8,128)(2,1)}, u32[]{:S(2)}, u32[]{:S(2)}) collective-permute-start(bf16[256,1024]{1,0:T(8,128)(2,1)} %param.21), channel_id=1, source_target_pairs={{0,3},{1,0},{2,1},{3,2},{4,7},{5,4},{6,5},{7,6},{8,11},{9,8},{10,9... | collective-permute-start | bytes 1572872 | tf_op jit(solution)/shard_map/ppermute | solution.py:163
  32.1 84.4 %copy-start.16 = (s32[1024]{0:T(1024)}, s32[1024]{0:T(1024)S(1)}, u32[]{:S(2)}) copy-start(s32[1024]{0:T(1024)S(1)} %pad_clamp_fusion.1) | copy-start | bytes 12292
  164.7 21.5 %copy-start.18 = (s32[34]{0:T(128)S(1)}, s32[34]{0:T(128)}, u32[]{:S(2)}) copy-start(s32[34]{0:T(128)} %copy-done.17) | copy-start | bytes 412
  235.0 11.6 %collective-permute-start.1 = (bf16[2,2,2,2,2,4,128,64]{6,7,5,4,3,2,1,0:T(8,128)(2,1)}, bf16[2,2,2,2,2,4,128,64]{6,7,5,4,3,2,1,0:T(8,128)(2,1)}, u32[]{:S(2)}, u32[]{:S(2)}) collective-permute-start(bf16[2,2,2,2,2,4,128,64]{6,7,5,4,3,2,1,0:T(8,128)(2,1)} %fusion.22), channel_id=1, source_target_pairs={{0,4},{4,0},{8,12},{12,8},{16,20},{20,16},{24,28},{28,24},{32,36},... | collective-permute-start | bytes 6291464 | tf_op jit(solution)/shard_map/ppermute | solution.py:148
  243.0 1.4 collective-permute-start
  244.6 6.5 %collective-permute-start.2 = (f32[2,2,2,2,4,128,2]{5,4,3,2,1,0,6:T(4,128)S(1)}, f32[2,2,2,2,4,128,2]{5,4,3,2,1,0,6:T(4,128)S(1)}, u32[]{:S(2)}, u32[]{:S(2)}) collective-permute-start(f32[2,2,2,2,4,128,2]{5,4,3,2,1,0,6:T(4,128)S(1)} %get-tuple-element.30), channel_id=1, source_target_pairs={{0,8},{4,12},{8,0},{12,4},{16,24},{20,28},{24,16},{28,20},{32,40},... | collective-permute-start | bytes 196616 | tf_op jit(solution)/shard_map/ppermute | solution.py:149
  250.7 25.3 %collective-permute-start.3 = (bf16[2,2,2,2,4,128,64]{5,6,4,3,2,1,0:T(8,128)(2,1)S(1)}, bf16[2,2,2,2,4,128,64]{5,6,4,3,2,1,0:T(8,128)(2,1)S(1)}, u32[]{:S(2)}, u32[]{:S(2)}) collective-permute-start(bf16[2,2,2,2,4,128,64]{5,6,4,3,2,1,0:T(8,128)(2,1)S(1)} %fusion.37), channel_id=1, source_target_pairs={{0,8},{4,12},{8,0},{12,4},{16,24},{20,28},{24,16},{28,20},{32,40},... | collective-permute-start | bytes 3145736 | tf_op jit(solution)/shard_map/ppermute | solution.py:148
  251.1 4.0 collective-permute-start.4
  255.1 22.4 %collective-permute-start.6 = (f32[2,2,4,128,2]{3,2,1,0,4:T(4,128)S(1)}, f32[2,2,4,128,2]{3,2,1,0,4:T(4,128)S(1)}, u32[]{:S(2)}, u32[]{:S(2)}) collective-permute-start(f32[2,2,4,128,2]{3,2,1,0,4:T(4,128)S(1)} %get-tuple-element.36), channel_id=1, source_target_pairs={{0,16},{4,20},{8,24},{12,28},{16,0},{20,4},{24,8},{28,12},{32,48},... | collective-permute-start | bytes 49160 | tf_op jit(solution)/shard_map/ppermute | solution.py:149
  276.8 13.1 %collective-permute-start.5 = (bf16[2,2,2,4,128,64]{4,5,3,2,1,0:T(8,128)(2,1)S(1)}, bf16[2,2,2,4,128,64]{4,5,3,2,1,0:T(8,128)(2,1)S(1)}, u32[]{:S(2)}, u32[]{:S(2)}) collective-permute-start(bf16[2,2,2,4,128,64]{4,5,3,2,1,0:T(8,128)(2,1)S(1)} %fusion.54), channel_id=1, source_target_pairs={{0,32},{4,36},{8,40},{12,44},{16,48},{20,52},{24,56},{28,60},{32,0... | collective-permute-start | bytes 1572872 | tf_op jit(solution)/shard_map/ppermute | solution.py:148
  277.6 13.4 %collective-permute-start.8 = (f32[2,4,128,2]{2,1,0,3:T(4,128)S(1)}, f32[2,4,128,2]{2,1,0,3:T(4,128)S(1)}, u32[]{:S(2)}, u32[]{:S(2)}) collective-permute-start(f32[2,4,128,2]{2,1,0,3:T(4,128)S(1)} %get-tuple-element.40), channel_id=1, source_target_pairs={{0,64},{4,68},{8,72},{12,76},{16,80},{20,84},{24,88},{28,92},{32,9... | collective-permute-start | bytes 24584 | tf_op jit(solution)/shard_map/ppermute | solution.py:149
  290.1 8.0 %collective-permute-start.7 = (bf16[2,2,4,128,64]{3,4,2,1,0:T(8,128)(2,1)S(1)}, bf16[2,2,4,128,64]{3,4,2,1,0:T(8,128)(2,1)S(1)}, u32[]{:S(2)}, u32[]{:S(2)}) collective-permute-start(bf16[2,2,4,128,64]{3,4,2,1,0:T(8,128)(2,1)S(1)} %fusion.60), channel_id=1, source_target_pairs={{0,16},{4,20},{8,24},{12,28},{16,0},{20,4},{24,8},{28,12},{32,48},... | collective-permute-start | bytes 786440 | tf_op jit(solution)/shard_map/ppermute | solution.py:148
  291.1 17.7 %collective-permute-start.10 = (f32[4,128,2]{1,0,2:T(4,128)S(1)}, f32[4,128,2]{1,0,2:T(4,128)S(1)}, u32[]{:S(2)}, u32[]{:S(2)}) collective-permute-start(f32[4,128,2]{1,0,2:T(4,128)S(1)} %get-tuple-element.47), channel_id=1, source_target_pairs={{0,128},{4,132},{8,136},{12,140},{16,144},{20,148},{24,152},{28,15... | collective-permute-start | bytes 12296 | tf_op jit(solution)/shard_map/ppermute | solution.py:149
  298.3 7.4 %collective-permute-start.9 = (bf16[2,4,128,64]{2,3,1,0:T(8,128)(2,1)S(1)}, bf16[2,4,128,64]{2,3,1,0:T(8,128)(2,1)S(1)}, u32[]{:S(2)}, u32[]{:S(2)}) collective-permute-start(bf16[2,4,128,64]{2,3,1,0:T(8,128)(2,1)S(1)} %fusion.69), channel_id=1, source_target_pairs={{0,64},{4,68},{8,72},{12,76},{16,80},{20,84},{24,88},{28,92},{32,9... | collective-permute-start | bytes 393224 | tf_op jit(solution)/shard_map/ppermute | solution.py:148
  305.8 9.0 %collective-permute-start.11 = (bf16[4,128,64]{1,2,0:T(8,128)(2,1)S(1)}, bf16[4,128,64]{1,2,0:T(8,128)(2,1)S(1)}, u32[]{:S(2)}, u32[]{:S(2)}) collective-permute-start(bf16[4,128,64]{1,2,0:T(8,128)(2,1)S(1)} %fusion.73), channel_id=1, source_target_pairs={{0,128},{4,132},{8,136},{12,140},{16,144},{20,148},{24,152},{28,15... | collective-permute-start | bytes 196616 | tf_op jit(solution)/shard_map/ppermute | solution.py:148
  314.8 6.7 %collective-permute-start.12 = (bf16[128,256]{0,1:T(8,128)(2,1)S(1)}, bf16[128,256]{0,1:T(8,128)(2,1)S(1)}, u32[]{:S(2)}, u32[]{:S(2)}) collective-permute-start(bf16[128,256]{0,1:T(8,128)(2,1)S(1)} %bitcast.233), channel_id=1, source_target_pairs={{0,1},{1,2},{2,3},{3,0},{4,5},{5,6},{6,7},{7,4},{8,9},{9,10},{10,1... | collective-permute-start | bytes 196616 | tf_op jit(solution)/shard_map/ppermute | solution.py:163
  316.3 5.8 %collective-permute-start.13 = (bf16[128,256]{0,1:T(8,128)(2,1)S(1)}, bf16[128,256]{0,1:T(8,128)(2,1)S(1)}, u32[]{:S(2)}, u32[]{:S(2)}) collective-permute-start(bf16[128,256]{0,1:T(8,128)(2,1)S(1)} %bitcast.234), channel_id=1, source_target_pairs={{0,2},{1,3},{2,0},{3,1},{4,6},{5,7},{6,4},{7,5},{8,10},{9,11},{10,... | collective-permute-start | bytes 196616 | tf_op jit(solution)/shard_map/ppermute | solution.py:163
  319.1 4.3 collective-permute-start.14
  393.9 56.8 %all-to-all-start.1 = ((bf16[64,1,10,1024]{3,2,1,0:T(8,128)(2,1)}), bf16[64,1,10,1024]{3,2,1,0:T(8,128)(2,1)S(1)}, u32[]{:S(2)}, u32[]{:S(2)}) async-start(bf16[64,1,10,1024]{3,2,1,0:T(8,128)(2,1)} %copy.130), calls=%async_computation.1 | async-start | bytes 4194304 | tf_op jit(solution)/shard_map/all_to_all | solution.py:207
  399.5 75.8 %reduce-scatter.2.cloned.1.call-start = ((), (), s32[]{:S(2)}) async-start(), calls=%async_computation.4 | async-start | bytes 327680 | tf_op jit(solution)/shard_map/reduce_scatter | solution.py:217
  (20 other events, 98.2 us)
Sparse Core Ops, SparseCore 0:
  10.1 80.6 all-gather.1
  456.1 19.1 reduce-scatter.1
where the time goes:
time: 488 us; the launch traced here: 484 us
  waiting for transfers between devices  173 us (35%)
  local copies, waits for them, and re-layouts  87.9 us (18%)
  matrix products  77.9 us (16%)
  blocking collectives  58.4 us (12%)
  other arithmetic  37.1 us (8%)
  starting transfers between devices  35 us (7%)
  between operations  14.4 us (3%)
    all_to_all x1, blocking collectives, shards(): lax.all_to_all(outgoing, 'seq', split_axis=0, concat_axis=0, tiled=True)  58.4 us
    all_gather x1, waiting for transfers between devices, shards(): lax.all_gather(queries, 'seq', axis=0, tiled=True)  56.6 us
    all_to_all x1, waiting for transfers between devices, shards(): lax.all_to_all(produced.astype(jnp.bfloat16), 'seq', split_axis=0, concat...  47.3 us
    ppermute x6, waiting for transfers between devices, shards(): lax.ppermute(send_acc.astype(jnp.bfloat16), 'seq', pairs)  44.2 us
    reshape x2, local copies, waits for them, and re-layouts, shards(): lax.all_gather(queries, 'seq', axis=0, tiled=True)  25.7 us
    dot_general x1, matrix products, shards(): jnp.einsum('br,bhqd->rhqd', weights, acc_block * factor[..., None], preci...  25.1 us
    dot_general x1, matrix products, shards(): jnp.einsum('bhqk,bkhd->bhqd', probs.astype(jnp.bfloat16), values, preferr...  21.5 us
    reduce_scatter x1, waiting for transfers between devices, shards(): lax.psum_scatter(mixture.astype(jnp.bfloat16), 'tp', scatter_dimension=1,...  19.3 us
  transfers between devices with their start and end apart: 21, of which 12 were waited for; matrix products, arithmetic and copies ran while one was open for 37% of the time, Pallas kernels for 0%

commit v1 on v0

--- a/solution.py
+++ b/solution.py
@@ -1,3 +1,4 @@
+import functools
 import jax
 import jax.numpy as jnp
 from jax import lax
@@ -11,6 +12,17 @@
 SPAN_DEVS = 4
 CAP = 10
 NEGATIVE = -1e30
+
+
+def supply_all_layers_all(field, peer_axis):
+    formed = lax.psum(1, peer_axis)
+    arr_now = jnp.stack(formed * [field])
+    response = lax.all_to_all(arr_now, peer_axis, 0, 0)
+    latest = jnp.concatenate(response, axis=0)
+    return latest
+
+
+group_the_trees = functools.partial(supply_all_layers_all, peer_axis="seq")
 
 
 def passed_along(value, axis, steps):
@@ -102,9 +114,7 @@
     values = jnp.concatenate(
         [cache_v.reshape(page_count, PAGE, local_heads, DH), new_values[None]], axis=0
     )
-    everyone = lax.all_gather(queries, "seq", axis=0, tiled=True).reshape(
-        request_total, span_rows, local_heads, DH
-    )
+    everyone = group_the_trees(queries).reshape(request_total, span_rows, local_heads, DH)
     rows = everyone[jnp.maximum(owners, 0)]
     scores = jnp.einsum("bqhd,bkhd->bhqk", rows, keys, preferred_element_type=jnp.float32) * DH ** (
         -0.5

time: 488 us -> 512 us (1.049)
  waiting for transfers between devices: 173 us -> 196 us
  starting transfers between devices: 35 us -> 40.4 us
    all_to_all x0 -> x1, waiting for transfers between devices: none -> 73.1 us  [supply_all_layers_all(): response = lax.all_to_all(arr_now, peer_axis, 0, 0)]
    all_gather x1 -> x0, waiting for transfers between devices: 56.6 us -> none  [shards(): lax.all_gather(queries, 'seq', axis=0, tiled=True)]
    reshape x2 -> x0, local copies, waits for them, and re-layouts: 25.7 us -> none  [shards(): lax.all_gather(queries, 'seq', axis=0, tiled=True)]
    another operation x1 -> x4, local copies, waits for them, and re-layouts: 0.01 us -> 17.1 us  [the longest x2 14.1 us: shards(): group_the_trees(queries).reshape(request_total, span_rows, local_heads, DH)]
    all_to_all x0 -> x1, starting transfers between devices: none -> 12.3 us  [supply_all_layers_all(): response = lax.all_to_all(arr_now, peer_axis, 0, 0)]
    all_to_all x0 -> x1, local copies, waits for them, and re-layouts: none -> 6.91 us  [supply_all_layers_all(): response = lax.all_to_all(arr_now, peer_axis, 0, 0)]
    ppermute x6, starting transfers between devices: 10.2 us -> 4.81 us  [shards(): got_stats = lax.ppermute(send_stats, 'seq', pairs)]
    ppermute x6, waiting for transfers between devices: 44.2 us -> 49.5 us  [shards(): lax.ppermute(send_acc.astype(jnp.bfloat16), 'seq', pairs)]
  transfers between devices with their start and end apart: 21 -> 21, of which waited for: 12 -> 13; matrix products, arithmetic and copies ran while one was open for 37% -> 34% of each run, Pallas kernels for 0% -> 0%
where the time goes in v1:
time: 512 us; the launch traced here: 507 us
  waiting for transfers between devices  196 us (38%)
  local copies, waits for them, and re-layouts  84.7 us (17%)
  matrix products  77 us (15%)
  blocking collectives  57.3 us (11%)
  starting transfers between devices  40.4 us (8%)
  other arithmetic  37.5 us (7%)
  between operations  14.5 us (3%)
    all_to_all x1, waiting for transfers between devices, supply_all_layers_all(): response = lax.all_to_all(arr_now, peer_axis, 0, 0)  73.1 us
    all_to_all x1, blocking collectives, shards(): lax.all_to_all(outgoing, 'seq', split_axis=0, concat_axis=0, tiled=True)  57.3 us
    ppermute x6, waiting for transfers between devices, shards(): lax.ppermute(send_acc.astype(jnp.bfloat16), 'seq', pairs)  49.5 us
    all_to_all x1, waiting for transfers between devices, shards(): lax.all_to_all(produced.astype(jnp.bfloat16), 'seq', split_axis=0, concat...  47.3 us
    dot_general x1, matrix products, shards(): jnp.einsum('br,bhqd->rhqd', weights, acc_block * factor[..., None], preci...  24.9 us
    dot_general x1, matrix products, shards(): jnp.einsum('bhqk,bkhd->bhqd', probs.astype(jnp.bfloat16), values, preferr...  21.5 us
    reduce_scatter x1, waiting for transfers between devices, shards(): lax.psum_scatter(mixture.astype(jnp.bfloat16), 'tp', scatter_dimension=1,...  19.3 us
    reduce_sum x1, other arithmetic, shards(): l_block = jnp.sum(probs, axis=-1)  17.9 us
  transfers between devices with their start and end apart: 21, of which 13 were waited for; matrix products, arithmetic and copies ran while one was open for 34% of the time, Pallas kernels for 0%

profile of v1, /device:TPU:2, one launch (start us, length us, event | category | flops | bytes accessed | tf_op | source)
XLA Modules:
  0.0 506.8 jit_solution(16037547418997433374)
XLA Ops:
  12.3 12.3 %all-to-all-start = ((bf16[64,128,256]{1,2,0:T(8,128)(2,1)}), bf16[64,128,256]{1,2,0:T(8,128)(2,1)}, u32[]{:S(2)}, u32[]{:S(2)}) async-start(bf16[64,128,256]{1,2,0:T(8,128)(2,1)} %stack.36), calls=%async_computation | async-start | bytes 8388608 | tf_op jit(solution)/shard_map/all_to_all | solution.py:20
  38.9 4.1 copy.115
  47.6 73.1 %all-to-all-done = bf16[64,128,256]{1,2,0:T(8,128)(2,1)} async-done(((bf16[64,128,256]{1,2,0:T(8,128)(2,1)}), bf16[64,128,256]{1,2,0:T(8,128)(2,1)}, u32[]{:S(2)}, u32[]{:S(2)}) %all-to-all-start) | async-done | bytes 4194336 | tf_op jit(solution)/shard_map/all_to_all | solution.py:20
  120.7 6.9 %copy.111 = bf16[64,128,256]{1,0,2:T(8,128)(2,1)} copy(bf16[64,128,256]{1,2,0:T(8,128)(2,1)} %all-to-all-done) | data formatting | bytes 8388608 | tf_op jit(solution)/shard_map/all_to_all | solution.py:20
  127.6 7.5 %reshape_reshape.6 = bf16[16,512,4,64]{1,0,3,2:T(8,128)(2,1)} reshape(bf16[64,128,256]{1,0,2:T(8,128)(2,1)} %copy.111) | data formatting | bytes 8388608 | tf_op jit(solution)/shard_map/reshape;reshape | solution.py:117
  135.2 6.6 %copy.112 = bf16[16,512,4,64]{1,3,2,0:T(8,128)(2,1)} copy(bf16[16,512,4,64]{1,0,3,2:T(8,128)(2,1)} %reshape_reshape.6) | data formatting | bytes 8388608 | tf_op jit(solution)/shard_map/reshape;reshape | solution.py:117
  141.7 7.5 %gather_fusion.1 = bf16[34,512,4,64]{1,3,2,0:T(8,128)(2,1)} fusion(bf16[16,512,4,64]{1,3,2,0:T(8,128)(2,1)} %copy.112, s32[1024]{0:T(1024)S(1)} %pad_clamp_fusion.1), kind=kCustom, calls=%fused_computation.1 | custom fusion | bytes 17825928 | tf_op jit(solution)/shard_map/gather | solution.py:118
  149.2 17.1 %fusion = (f32[34,4,512]{2,1,0:T(4,128)S(1)}, f32[34,4,512,128]{2,3,1,0:T(8,128)}) fusion(pred[34,512,128]{1,2,0:T(8,128)(4,1)S(1)} %pad_add_fusion, bf16[34,512,4,64]{1,3,2,0:T(8,128)(2,1)} %gather_fusion.1, bf16[1,128,4,64]{1,3,2,0:T(8,128)(2,1)S(1)} %bitcast.240, bf16[33,128,4,64]{1,3,2,0:T(8,128)(2,1)} %bitcast.225), kind=kOutput, calls=%fused_computation.8 | convolution fusion | flops 1168633856 | bytes 49299456 | tf_op jit(solution)/shard_map/bqhd,bkhd->bhqk/dot_general | solution.py:119
  166.3 17.9 %fusion.1 = f32[34,4,512]{2,1,0:T(4,128)} fusion(f32[34,4,512,128]{2,3,1,0:T(8,128)} %get-tuple-element.56, f32[34,4,512]{2,1,0:T(4,128)S(1)} %get-tuple-element.55, pred[34,512,128]{1,2,0:T(8,128)(4,1)S(1)} %pad_add_fusion), kind=kLoop, calls=%fused_computation.9 | loop fusion | flops 44494848 | bytes 38436864 | tf_op jit(solution)/shard_map/reduce_sum | solution.py:125
  190.3 21.5 %broadcast_multiply_fusion = f32[34,4,512,64]{2,3,1,0:T(8,128)} fusion(f32[34,4,512]{2,1,0:T(4,128)S(1)} %bitcast.234, f32[34,4,512,128]{2,3,1,0:T(8,128)} %get-tuple-element.56, f32[34,4,512]{2,1,0:T(4,128)S(1)} %get-tuple-element.55, pred[34,512,128]{1,2,0:T(8,128)(4,1)S(1)} %pad_add_fusion, bf16[1,128,4,64]{1,3,2,0:T(8,128)(2,1)S(1)} %bitcast.241, ...), kind=kOutput, calls=%fused_computation.19 | convolution fusion | flops 1194328064 | bytes 58490880 | tf_op jit(solution)/shard_map/bhqk,bkhd->bhqd/dot_general | solution.py:126
  211.8 24.9 %fusion.3 = f32[16,4,512,64]{2,0,3,1:T(8,128)} fusion(f32[34,4,512,64]{2,3,1,0:T(8,128)} %broadcast_multiply_fusion, s32[34]{0:T(128)S(1)} %copy-done.20), kind=kOutput, calls=%fused_computation.11 | convolution fusion | flops 855638528 | bytes 26214536 | tf_op jit(solution)/shard_map/br,bhqd->rhqd/dot_general | solution.py:133
  236.7 10.1 %reshape.407 = f32[16,4,4,128,64]{3,2,0,4,1:T(4,128)} reshape(f32[16,4,512,64]{2,0,3,1:T(8,128)} %fusion.3) | data formatting | bytes 16777216 | tf_op jit(solution)/shard_map/reshape | solution.py:139
  246.8 8.2 %copy.121 = f32[16,4,4,128,64]{3,4,2,1,0:T(8,128)S(1)} copy(f32[16,4,4,128,64]{3,1,0,4,2:T(4,128)} %bitcast.219) | data formatting | bytes 16777216 | tf_op jit(solution)/shard_map/transpose | solution.py:138
  270.5 4.0 fusion.14
  276.8 3.4 collective-permute-done.4
  282.6 17.5 %collective-permute-done.3 = bf16[2,2,2,2,4,128,64]{5,6,4,3,2,1,0:T(8,128)(2,1)S(1)} collective-permute-done((bf16[2,2,2,2,4,128,64]{5,6,4,3,2,1,0:T(8,128)(2,1)S(1)}, bf16[2,2,2,2,4,128,64]{5,6,4,3,2,1,0:T(8,128)(2,1)S(1)}, u32[]{:S(2)}, u32[]{:S(2)}) %collective-permute-start.3) | collective-permute-done | bytes 1048608 | tf_op jit(solution)/shard_map/ppermute | solution.py:158
  302.1 11.8 %collective-permute-done.5 = bf16[2,2,2,4,128,64]{4,5,3,2,1,0:T(8,128)(2,1)S(1)} collective-permute-done((bf16[2,2,2,4,128,64]{4,5,3,2,1,0:T(8,128)(2,1)S(1)}, bf16[2,2,2,4,128,64]{4,5,3,2,1,0:T(8,128)(2,1)S(1)}, u32[]{:S(2)}, u32[]{:S(2)}) %collective-permute-start.5) | collective-permute-done | bytes 524320 | tf_op jit(solution)/shard_map/ppermute | solution.py:158
  316.7 5.7 %collective-permute-done.7 = bf16[2,2,4,128,64]{3,4,2,1,0:T(8,128)(2,1)S(1)} collective-permute-done((bf16[2,2,4,128,64]{3,4,2,1,0:T(8,128)(2,1)S(1)}, bf16[2,2,4,128,64]{3,4,2,1,0:T(8,128)(2,1)S(1)}, u32[]{:S(2)}, u32[]{:S(2)}) %collective-permute-start.7) | collective-permute-done | bytes 262176 | tf_op jit(solution)/shard_map/ppermute | solution.py:158
  322.6 7.0 %collective-permute-done.9 = bf16[2,4,128,64]{2,3,1,0:T(8,128)(2,1)S(1)} collective-permute-done((bf16[2,4,128,64]{2,3,1,0:T(8,128)(2,1)S(1)}, bf16[2,4,128,64]{2,3,1,0:T(8,128)(2,1)S(1)}, u32[]{:S(2)}, u32[]{:S(2)}) %collective-permute-start.9) | collective-permute-done | bytes 131104 | tf_op jit(solution)/shard_map/ppermute | solution.py:158
  331.0 7.6 %collective-permute-done.11 = bf16[4,128,64]{1,2,0:T(8,128)(2,1)S(1)} collective-permute-done((bf16[4,128,64]{1,2,0:T(8,128)(2,1)S(1)}, bf16[4,128,64]{1,2,0:T(8,128)(2,1)S(1)}, u32[]{:S(2)}, u32[]{:S(2)}) %collective-permute-start.11) | collective-permute-done | bytes 65568 | tf_op jit(solution)/shard_map/ppermute | solution.py:158
  351.5 57.3 %all_to_all.15 = bf16[64,1,10,1024]{3,2,1,0:T(8,128)(2,1)S(1)} all-to-all(bf16[64,1,10,1024]{3,2,1,0:T(8,128)(2,1)S(1)} %bitcast.223), channel_id=1, replica_groups=mesh['seq'=64,'tp'=4] {'seq'}, dimensions={0} | all-to-all | bytes 2621440 | tf_op jit(solution)/shard_map/all_to_all | solution.py:205
  416.9 5.6 %all-to-all-start.2 = ((bf16[64,1,10,1024]{3,2,1,0:T(8,128)(2,1)}), bf16[64,1,10,1024]{3,2,1,0:T(8,128)(2,1)S(1)}, u32[]{:S(2)}, u32[]{:S(2)}) async-start(bf16[64,1,10,1024]{3,2,1,0:T(8,128)(2,1)} %copy.133), calls=%async_computation.2 | async-start | bytes 4194304 | tf_op jit(solution)/shard_map/all_to_all | solution.py:217
  426.4 47.3 %all-to-all-done.2 = bf16[64,1,10,1024]{3,2,1,0:T(8,128)(2,1)S(1)} async-done(((bf16[64,1,10,1024]{3,2,1,0:T(8,128)(2,1)}), bf16[64,1,10,1024]{3,2,1,0:T(8,128)(2,1)S(1)}, u32[]{:S(2)}, u32[]{:S(2)}) %all-to-all-start.2) | async-done | bytes 1310752 | tf_op jit(solution)/shard_map/all_to_all | solution.py:217
  479.0 19.3 %reduce-scatter.2.cloned.1.call-done = bf16[128,256]{1,0:T(8,128)(2,1)} async-done(((bf16[128,1024]{1,0:T(8,128)(2,1)}), bf16[128,256]{1,0:T(8,128)(2,1)}) %reduce-scatter.2.cloned.1.call-update) | async-done | bytes 65552 | tf_op jit(solution)/shard_map/reduce_scatter | solution.py:227
  (199 shorter events, 88.3 us)
Async XLA Ops:
  6.5 407.3 %copy-start = (bf16[1,352,1024]{2,1,0:T(8,128)(2,1)S(1)}, bf16[1,352,1024]{2,1,0:T(8,128)(2,1)}, u32[]{:S(2)}) copy-start(bf16[1,352,1024]{2,1,0:T(8,128)(2,1)} %param.27) | copy-start | bytes 2162692
  12.3 108.5 %all-to-all-start = ((bf16[64,128,256]{1,2,0:T(8,128)(2,1)}), bf16[64,128,256]{1,2,0:T(8,128)(2,1)}, u32[]{:S(2)}, u32[]{:S(2)}) async-start(bf16[64,128,256]{1,2,0:T(8,128)(2,1)} %stack.36), calls=%async_computation | async-start | bytes 8388608 | tf_op jit(solution)/shard_map/all_to_all | solution.py:20
  24.6 235.6 %collective-permute-start.15 = (bf16[256,1024]{1,0:T(8,128)(2,1)}, bf16[256,1024]{1,0:T(8,128)(2,1)}, u32[]{:S(2)}, u32[]{:S(2)}) collective-permute-start(bf16[256,1024]{1,0:T(8,128)(2,1)} %param.21), channel_id=1, source_target_pairs={{0,1},{1,2},{2,3},{3,0},{4,5},{5,6},{6,7},{7,4},{8,9},{9,10},{10,1... | collective-permute-start | bytes 1572872 | tf_op jit(solution)/shard_map/ppermute | solution.py:173
  26.3 234.0 %collective-permute-start.16 = (bf16[256,1024]{1,0:T(8,128)(2,1)}, bf16[256,1024]{1,0:T(8,128)(2,1)}, u32[]{:S(2)}, u32[]{:S(2)}) collective-permute-start(bf16[256,1024]{1,0:T(8,128)(2,1)} %param.21), channel_id=1, source_target_pairs={{0,2},{1,3},{2,0},{3,1},{4,6},{5,7},{6,4},{7,5},{8,10},{9,11},{10,... | collective-permute-start | bytes 1572872 | tf_op jit(solution)/shard_map/ppermute | solution.py:173
  29.2 231.1 %collective-permute-start.17 = (bf16[256,1024]{1,0:T(8,128)(2,1)}, bf16[256,1024]{1,0:T(8,128)(2,1)}, u32[]{:S(2)}, u32[]{:S(2)}) collective-permute-start(bf16[256,1024]{1,0:T(8,128)(2,1)} %param.21), channel_id=1, source_target_pairs={{0,3},{1,0},{2,1},{3,2},{4,7},{5,4},{6,5},{7,6},{8,11},{9,8},{10,9... | collective-permute-start | bytes 1572872 | tf_op jit(solution)/shard_map/ppermute | solution.py:173
  45.4 96.3 %copy-start.18 = (s32[1024]{0:T(1024)}, s32[1024]{0:T(1024)S(1)}, u32[]{:S(2)}) copy-start(s32[1024]{0:T(1024)S(1)} %pad_clamp_fusion.1) | copy-start | bytes 12292
  190.3 21.5 %copy-start.20 = (s32[34]{0:T(128)S(1)}, s32[34]{0:T(128)}, u32[]{:S(2)}) copy-start(s32[34]{0:T(128)} %copy-done.19) | copy-start | bytes 412
  260.1 10.3 %collective-permute-start.1 = (bf16[2,2,2,2,2,4,128,64]{6,7,5,4,3,2,1,0:T(8,128)(2,1)}, bf16[2,2,2,2,2,4,128,64]{6,7,5,4,3,2,1,0:T(8,128)(2,1)}, u32[]{:S(2)}, u32[]{:S(2)}) collective-permute-start(bf16[2,2,2,2,2,4,128,64]{6,7,5,4,3,2,1,0:T(8,128)(2,1)} %fusion.22), channel_id=1, source_target_pairs={{0,4},{4,0},{8,12},{12,8},{16,20},{20,16},{24,28},{28,24},{32,36},... | collective-permute-start | bytes 6291464 | tf_op jit(solution)/shard_map/ppermute | solution.py:158
  268.0 1.6 collective-permute-start
  269.7 6.5 %collective-permute-start.2 = (f32[2,2,2,2,4,128,2]{5,4,3,2,1,0,6:T(4,128)S(1)}, f32[2,2,2,2,4,128,2]{5,4,3,2,1,0,6:T(4,128)S(1)}, u32[]{:S(2)}, u32[]{:S(2)}) collective-permute-start(f32[2,2,2,2,4,128,2]{5,4,3,2,1,0,6:T(4,128)S(1)} %get-tuple-element.30), channel_id=1, source_target_pairs={{0,8},{4,12},{8,0},{12,4},{16,24},{20,28},{24,16},{28,20},{32,40},... | collective-permute-start | bytes 196616 | tf_op jit(solution)/shard_map/ppermute | solution.py:159
  274.7 25.4 %collective-permute-start.3 = (bf16[2,2,2,2,4,128,64]{5,6,4,3,2,1,0:T(8,128)(2,1)S(1)}, bf16[2,2,2,2,4,128,64]{5,6,4,3,2,1,0:T(8,128)(2,1)S(1)}, u32[]{:S(2)}, u32[]{:S(2)}) collective-permute-start(bf16[2,2,2,2,4,128,64]{5,6,4,3,2,1,0:T(8,128)(2,1)S(1)} %fusion.37), channel_id=1, source_target_pairs={{0,8},{4,12},{8,0},{12,4},{16,24},{20,28},{24,16},{28,20},{32,40},... | collective-permute-start | bytes 3145736 | tf_op jit(solution)/shard_map/ppermute | solution.py:158
  276.2 4.0 collective-permute-start.4
  280.2 21.4 %collective-permute-start.6 = (f32[2,2,4,128,2]{3,2,1,0,4:T(4,128)S(1)}, f32[2,2,4,128,2]{3,2,1,0,4:T(4,128)S(1)}, u32[]{:S(2)}, u32[]{:S(2)}) collective-permute-start(f32[2,2,4,128,2]{3,2,1,0,4:T(4,128)S(1)} %get-tuple-element.36), channel_id=1, source_target_pairs={{0,16},{4,20},{8,24},{12,28},{16,0},{20,4},{24,8},{28,12},{32,48},... | collective-permute-start | bytes 49160 | tf_op jit(solution)/shard_map/ppermute | solution.py:159
  300.8 13.1 %collective-permute-start.5 = (bf16[2,2,2,4,128,64]{4,5,3,2,1,0:T(8,128)(2,1)S(1)}, bf16[2,2,2,4,128,64]{4,5,3,2,1,0:T(8,128)(2,1)S(1)}, u32[]{:S(2)}, u32[]{:S(2)}) collective-permute-start(bf16[2,2,2,4,128,64]{4,5,3,2,1,0:T(8,128)(2,1)S(1)} %fusion.54), channel_id=1, source_target_pairs={{0,32},{4,36},{8,40},{12,44},{16,48},{20,52},{24,56},{28,60},{32,0... | collective-permute-start | bytes 1572872 | tf_op jit(solution)/shard_map/ppermute | solution.py:158
  301.7 14.8 %collective-permute-start.8 = (f32[2,4,128,2]{2,1,0,3:T(4,128)S(1)}, f32[2,4,128,2]{2,1,0,3:T(4,128)S(1)}, u32[]{:S(2)}, u32[]{:S(2)}) collective-permute-start(f32[2,4,128,2]{2,1,0,3:T(4,128)S(1)} %get-tuple-element.40), channel_id=1, source_target_pairs={{0,64},{4,68},{8,72},{12,76},{16,80},{20,84},{24,88},{28,92},{32,9... | collective-permute-start | bytes 24584 | tf_op jit(solution)/shard_map/ppermute | solution.py:159
  314.2 8.1 %collective-permute-start.7 = (bf16[2,2,4,128,64]{3,4,2,1,0:T(8,128)(2,1)S(1)}, bf16[2,2,4,128,64]{3,4,2,1,0:T(8,128)(2,1)S(1)}, u32[]{:S(2)}, u32[]{:S(2)}) collective-permute-start(bf16[2,2,4,128,64]{3,4,2,1,0:T(8,128)(2,1)S(1)} %fusion.60), channel_id=1, source_target_pairs={{0,16},{4,20},{8,24},{12,28},{16,0},{20,4},{24,8},{28,12},{32,48},... | collective-permute-start | bytes 786440 | tf_op jit(solution)/shard_map/ppermute | solution.py:158
  316.6 14.4 %collective-permute-start.10 = (f32[4,128,2]{1,0,2:T(4,128)S(1)}, f32[4,128,2]{1,0,2:T(4,128)S(1)}, u32[]{:S(2)}, u32[]{:S(2)}) collective-permute-start(f32[4,128,2]{1,0,2:T(4,128)S(1)} %get-tuple-element.47), channel_id=1, source_target_pairs={{0,128},{4,132},{8,136},{12,140},{16,144},{20,148},{24,152},{28,15... | collective-permute-start | bytes 12296 | tf_op jit(solution)/shard_map/ppermute | solution.py:159
  322.5 7.1 %collective-permute-start.9 = (bf16[2,4,128,64]{2,3,1,0:T(8,128)(2,1)S(1)}, bf16[2,4,128,64]{2,3,1,0:T(8,128)(2,1)S(1)}, u32[]{:S(2)}, u32[]{:S(2)}) collective-permute-start(bf16[2,4,128,64]{2,3,1,0:T(8,128)(2,1)S(1)} %fusion.69), channel_id=1, source_target_pairs={{0,64},{4,68},{8,72},{12,76},{16,80},{20,84},{24,88},{28,92},{32,9... | collective-permute-start | bytes 393224 | tf_op jit(solution)/shard_map/ppermute | solution.py:158
  329.7 8.9 %collective-permute-start.11 = (bf16[4,128,64]{1,2,0:T(8,128)(2,1)S(1)}, bf16[4,128,64]{1,2,0:T(8,128)(2,1)S(1)}, u32[]{:S(2)}, u32[]{:S(2)}) collective-permute-start(bf16[4,128,64]{1,2,0:T(8,128)(2,1)S(1)} %fusion.73), channel_id=1, source_target_pairs={{0,128},{4,132},{8,136},{12,140},{16,144},{20,148},{24,152},{28,15... | collective-permute-start | bytes 196616 | tf_op jit(solution)/shard_map/ppermute | solution.py:158
  338.6 6.9 %collective-permute-start.12 = (bf16[128,256]{0,1:T(8,128)(2,1)S(1)}, bf16[128,256]{0,1:T(8,128)(2,1)S(1)}, u32[]{:S(2)}, u32[]{:S(2)}) collective-permute-start(bf16[128,256]{0,1:T(8,128)(2,1)S(1)} %bitcast.235), channel_id=1, source_target_pairs={{0,1},{1,2},{2,3},{3,0},{4,5},{5,6},{6,7},{7,4},{8,9},{9,10},{10,1... | collective-permute-start | bytes 196616 | tf_op jit(solution)/shard_map/ppermute | solution.py:173
  340.2 5.8 %collective-permute-start.13 = (bf16[128,256]{0,1:T(8,128)(2,1)S(1)}, bf16[128,256]{0,1:T(8,128)(2,1)S(1)}, u32[]{:S(2)}, u32[]{:S(2)}) collective-permute-start(bf16[128,256]{0,1:T(8,128)(2,1)S(1)} %bitcast.236), channel_id=1, source_target_pairs={{0,2},{1,3},{2,0},{3,1},{4,6},{5,7},{6,4},{7,5},{8,10},{9,11},{10,... | collective-permute-start | bytes 196616 | tf_op jit(solution)/shard_map/ppermute | solution.py:173
  343.1 4.3 collective-permute-start.14
  416.9 56.8 %all-to-all-start.2 = ((bf16[64,1,10,1024]{3,2,1,0:T(8,128)(2,1)}), bf16[64,1,10,1024]{3,2,1,0:T(8,128)(2,1)S(1)}, u32[]{:S(2)}, u32[]{:S(2)}) async-start(bf16[64,1,10,1024]{3,2,1,0:T(8,128)(2,1)} %copy.133), calls=%async_computation.2 | async-start | bytes 4194304 | tf_op jit(solution)/shard_map/all_to_all | solution.py:217
  422.4 75.8 %reduce-scatter.2.cloned.1.call-start = ((), (), s32[]{:S(2)}) async-start(), calls=%async_computation.4 | async-start | bytes 327680 | tf_op jit(solution)/shard_map/reduce_scatter | solution.py:227
  (22 other events, 157.2 us)
Sparse Core Ops, SparseCore 0:
  479.1 19.1 reduce-scatter.1
